TPU v7x, 256 devices: a whole 4x4x8 slice. The times are simulated.
256 devices in a mesh: batch: 16 (over y_hi, z), gx: 4 (over y_lo, core), gy: 4 (over x).
Axes of the slice: x: 4, y: 4 (y_hi: 2, y_lo: 2; y = y_hi * 2 + y_lo), z: 8, core: 2. Of those that a mesh axis runs over, the one named last changes fastest.
Arguments:
- features: bfloat16 [1024, 64, 4, 256], P(('batch', 'gx'), 'gy'), parts along dimension 0, may hold values from -6 to 6
- conv_weight: bfloat16 [6912, 256], replicated, may hold values from -0.078125 to 0.078125
- down_weight: bfloat16 [2048, 512], replicated, may hold values from -0.125 to 0.125
- norm_gain: float32 [512], replicated, may hold values from 0.1 to 1.9
- qkv_weight: bfloat16 [512, 1536], replicated, may hold values from -0.25 to 0.25
- out_weight: bfloat16 [512, 512], replicated, may hold values from -0.25 to 0.25
- upstream: bfloat16 [512, 32, 2, 512], P(('batch', 'gx'), 'gy'), parts along dimension 0, may hold values from -6 to 6
Outputs:
- grad_features: bfloat16 [1024, 64, 4, 256], P(('batch', 'gx'), 'gy'), parts along dimension 0
- grad_conv: bfloat16 [110592, 256], P(('batch', 'gx', 'gy')), parts along dimension 0
- grad_down: bfloat16 [32768, 512], P(('batch', 'gx', 'gy')), parts along dimension 0
- grad_gain: float32 [8192], P(('batch', 'gx', 'gy')), parts along dimension 0
- grad_qkv: bfloat16 [8192, 1536], P(('batch', 'gx', 'gy')), parts along dimension 0
- grad_out: bfloat16 [8192, 512], P(('batch', 'gx', 'gy')), parts along dimension 0
There are 16 independent parts, one for each index of `batch`. A program takes and returns all parts, laid end to end along the dimension named above; an argument that names none is the same for every part. Nothing has to cross between parts.
All inputs are finite; a program needn't handle non-finite values.
Results may differ from a plain program's by a relative error of at most 0.02.
Values may be sent and summed in bfloat16 or wider, within the bound.
No kernel may reach another device: no remote copies, remote signals or barrier semaphores. Data moves between devices by JAX's collectives and lax.ppermute only.
A program may use at most 128 MiB of HBM per device.

v0:
```python
import jax
import jax.numpy as jnp
from jax import lax
from jax.sharding import PartitionSpec as P

H = 8
HD = 64


precise = lax.Precision.HIGHEST


def padded_2(block, sides, width):
    for axis, dim in sides:
        count = lax.axis_size(axis)
        forward = [(i, i + 1) for i in range(count - 1)]
        backward = [(target, source) for source, target in forward]
        low = lax.ppermute(
            lax.slice_in_dim(block, block.shape[dim] - width, None, axis=dim), axis, forward
        )
        high = lax.ppermute(lax.slice_in_dim(block, 0, width, axis=dim), axis, backward)
        block = jnp.concatenate([low, block, high], axis=dim)
    return block


def to_tokens(volume):
    extent_x, extent_y, extent_z, channels = volume.shape
    grid = volume.reshape(extent_x // 2, 2, extent_y // 2, 2, extent_z // 2, 2, channels)
    grid = grid.transpose(0, 2, 4, 1, 3, 5, 6)
    return grid.reshape(extent_x * extent_y * extent_z // 8, 8 * channels)


def from_tokens(matrix, extent_x, extent_y, extent_z):
    channels = matrix.shape[1] // 8
    grid = matrix.reshape(extent_x // 2, extent_y // 2, extent_z // 2, 2, 2, 2, channels)
    grid = grid.transpose(0, 3, 1, 4, 2, 5, 6)
    return grid.reshape(extent_x, extent_y, extent_z, channels)


def gather_patches(padded, extent_x, extent_y, extent_z, flipped):
    channels = padded.shape[3]
    pieces = []
    for offset_x in range(3):
        for offset_y in range(3):
            for offset_z in range(3):
                start_x = 2 - offset_x if flipped else offset_x
                start_y = 2 - offset_y if flipped else offset_y
                start_z = 2 - offset_z if flipped else offset_z
                pieces.append(
                    padded[
                        start_x : start_x + extent_x,
                        start_y : start_y + extent_y,
                        start_z : start_z + extent_z,
                    ]
                )
    joined = jnp.concatenate(pieces, axis=3)
    return joined.reshape(extent_x * extent_y * extent_z, 27 * channels)


def local(features, conv_weight, down_weight, norm_gain, qkv_weight, out_weight, upstream):
    extent_x, extent_y, extent_z, channels = features.shape
    model_width = out_weight.shape[0]
    voxels = extent_x * extent_y * extent_z
    score_scale = HD ** (-0.5)
    padded = padded_2(features, (("gx", 0), ("gy", 1)), 1)
    padded = jnp.pad(padded, ((0, 0), (0, 0), (1, 1), (0, 0)))
    patches = gather_patches(padded, extent_x, extent_y, extent_z, False)
    hidden = jnp.dot(patches, conv_weight, preferred_element_type=jnp.float32)
    gate_sig = jax.nn.sigmoid(hidden)
    activation = (hidden * gate_sig).astype(jnp.bfloat16)
    tokens_in = to_tokens(activation.reshape(extent_x, extent_y, extent_z, channels))
    tok_count = tokens_in.shape[0]
    trunk_rows = jnp.dot(tokens_in, down_weight, preferred_element_type=jnp.float32)
    mean_rows = jnp.mean(trunk_rows, axis=-1, keepdims=True)
    centred = trunk_rows - mean_rows
    inverse_std = lax.rsqrt(jnp.mean(centred * centred, axis=-1, keepdims=True) + 1e-05)
    normed = centred * inverse_std
    normed_b = (normed * norm_gain).astype(jnp.bfloat16)
    qkv_rows = jnp.dot(normed_b, qkv_weight, preferred_element_type=jnp.float32).astype(
        jnp.bfloat16
    )
    queries = qkv_rows[:, :model_width]
    local_keys = qkv_rows[:, model_width : 2 * model_width]
    local_values = qkv_rows[:, 2 * model_width :]
    all_keys, all_values = (
        lax.all_gather(local_keys, ("gx", "gy"), axis=0, tiled=True),
        lax.all_gather(local_values, ("gx", "gy"), axis=0, tiled=True),
    )
    queries_h = queries.reshape(tok_count, H, HD)
    keys_h = all_keys.reshape(-1, H, HD)
    values_h = all_values.reshape(-1, H, HD)
    scores = (
        jnp.einsum("ihe,jhe->hij", queries_h, keys_h, preferred_element_type=jnp.float32)
        * score_scale
    )
    exp_scores = jnp.exp(scores)
    totals = jnp.sum(exp_scores, axis=-1)
    attn_probs = exp_scores / totals[:, :, None]
    probs_b = attn_probs.astype(jnp.bfloat16)
    attended = jnp.einsum("hij,jhe->ihe", probs_b, values_h, preferred_element_type=jnp.float32)
    attended = attended.reshape(tok_count, model_width).astype(jnp.bfloat16)
    cotangent = upstream.reshape(tok_count, model_width)
    cot_float = cotangent.astype(jnp.float32)
    out_part = jnp.einsum("td,te->de", attended, cotangent, preferred_element_type=jnp.float32)
    d_attended = jnp.dot(cotangent, out_weight.T, preferred_element_type=jnp.float32).astype(
        jnp.bfloat16
    )
    d_att_h = d_attended.reshape(tok_count, H, HD)
    d_probs = jnp.einsum("ihe,jhe->hij", d_att_h, values_h, preferred_element_type=jnp.float32)
    d_probs = d_probs.astype(jnp.bfloat16).astype(jnp.float32)
    row_delta = jnp.sum(attn_probs * d_probs, axis=-1)
    d_scores = attn_probs * (d_probs - row_delta[:, :, None])
    d_queries = (
        jnp.einsum(
            "hij,jhe->ihe", d_scores, keys_h, precision=precise, preferred_element_type=jnp.float32
        )
        * score_scale
    )
    key_term = (
        jnp.einsum(
            "hij,ihe->jhe",
            d_scores,
            queries_h,
            precision=precise,
            preferred_element_type=jnp.float32,
        )
        * score_scale
    )
    value_term = jnp.einsum("hij,ihe->jhe", probs_b, d_att_h, preferred_element_type=jnp.float32)
    key_sums = lax.psum_scatter(
        jnp.concatenate(
            [
                key_term.reshape(tok_count * lax.axis_size(("gx", "gy")), model_width),
                value_term.reshape(tok_count * lax.axis_size(("gx", "gy")), model_width),
            ],
            axis=1,
        ).astype(jnp.bfloat16),
        ("gx", "gy"),
        scatter_dimension=0,
        tiled=True,
    ).astype(jnp.float32)
    d_keys = key_sums[:, :model_width].astype(jnp.bfloat16)
    d_values = key_sums[:, model_width:].astype(jnp.bfloat16)
    d_qkv = jnp.concatenate(
        [d_queries.reshape(tok_count, model_width).astype(jnp.bfloat16), d_keys, d_values], axis=1
    )
    qkv_part = jnp.einsum("td,te->de", normed_b, d_qkv, preferred_element_type=jnp.float32)
    d_normed = (
        jnp.dot(d_qkv, qkv_weight.T, preferred_element_type=jnp.float32)
        .astype(jnp.bfloat16)
        .astype(jnp.float32)
    )
    d_hat = d_normed * norm_gain
    gain_part = jnp.sum(d_normed * normed, axis=0)
    gain_sum = lax.psum_scatter(gain_part, ("gx", "gy"), scatter_dimension=0, tiled=True)
    d_trunk = cot_float + inverse_std * (
        d_hat
        - jnp.mean(d_hat, axis=-1, keepdims=True)
        - normed * jnp.mean(d_hat * normed, axis=-1, keepdims=True)
    )
    down_part = jnp.einsum(
        "tr,td->rd", tokens_in, d_trunk, precision=precise, preferred_element_type=jnp.float32
    )
    d_activation = jnp.dot(
        d_trunk, down_weight.T, precision=precise, preferred_element_type=jnp.float32
    ).astype(jnp.bfloat16)
    d_act_grid = (
        from_tokens(d_activation, extent_x, extent_y, extent_z)
        .reshape(voxels, channels)
        .astype(jnp.float32)
    )
    d_hidden = (d_act_grid * gate_sig * (1.0 + hidden * (1.0 - gate_sig))).astype(jnp.bfloat16)
    conv_part = jnp.einsum("vr,vc->rc", patches, d_hidden, preferred_element_type=jnp.float32)
    d_padded = padded_2(
        d_hidden.reshape(extent_x, extent_y, extent_z, channels), (("gx", 0), ("gy", 1)), 1
    )
    d_padded = jnp.pad(d_padded, ((0, 0), (0, 0), (1, 1), (0, 0)))
    d_patches = gather_patches(d_padded, extent_x, extent_y, extent_z, True)
    conv_flip = (
        conv_weight.reshape(27, channels, channels)
        .transpose(0, 2, 1)
        .reshape(27 * channels, channels)
    )
    grad_features = jnp.dot(d_patches, conv_flip, preferred_element_type=jnp.float32)
    grad_features = grad_features.reshape(extent_x, extent_y, extent_z, channels).astype(
        jnp.bfloat16
    )
    conv_sum, down_sum, qkv_sum, out_sum = (
        lax.psum_scatter(
            conv_part.astype(jnp.bfloat16), ("gx", "gy"), scatter_dimension=0, tiled=True
        ).astype(jnp.float32),
        lax.psum_scatter(
            down_part.astype(jnp.bfloat16), ("gx", "gy"), scatter_dimension=0, tiled=True
        ).astype(jnp.float32),
        lax.psum_scatter(
            qkv_part.astype(jnp.bfloat16), ("gx", "gy"), scatter_dimension=0, tiled=True
        ).astype(jnp.float32),
        lax.psum_scatter(
            out_part.astype(jnp.bfloat16), ("gx", "gy"), scatter_dimension=0, tiled=True
        ).astype(jnp.float32),
    )
    return (
        grad_features,
        conv_sum.astype(jnp.bfloat16),
        down_sum.astype(jnp.bfloat16),
        gain_sum,
        qkv_sum.astype(jnp.bfloat16),
        out_sum.astype(jnp.bfloat16),
    )


def solution(mesh):
    placed = (
        P(("batch", "gx"), "gy", None, None),
        P(),
        P(),
        P(),
        P(),
        P(),
        P(("batch", "gx"), "gy", None, None),
    )
    return jax.shard_map(
        local,
        mesh=mesh,
        in_specs=placed,
        out_specs=(
            P(("batch", "gx"), "gy", None, None),
            P(("batch", "gx", "gy"), None),
            P(("batch", "gx", "gy"), None),
            P(("batch", "gx", "gy")),
            P(("batch", "gx", "gy"), None),
            P(("batch", "gx", "gy"), None),
        ),
        check_vma=False,
    )
```

profile of v0, /device:TPU:1, one launch (start us, length us, event | category | flops | bytes accessed | tf_op | source)
XLA Modules:
  0.0 585.5 jit_solution(17432155267392307056)
XLA Ops:
  8.2 4.6 collective-permute-start
  18.1 3.1 collective-permute-start.2
  22.5 3.4 collective-permute-done.3
  58.3 22.7 %reshape.89 = bf16[1024,6912]{1,0:T(8,128)(2,1)} reshape(bf16[16,16,4,6912]{3,2,1,0:T(4,128)(2,1)} %slice_dynamic-update-slice_fusion.18) | data formatting | bytes 28311552 | tf_op jit(solution)/shard_map/reshape | solution.py:57
  81.1 10.9 %multiply_convert_fusion.2 = (bf16[1024,256]{1,0:T(8,128)(2,1)S(1)}, f32[1024,256]{1,0:T(8,128)}) fusion(bf16[1024,6912]{1,0:T(8,128)(2,1)} %reshape.89, bf16[6912,256]{1,0:T(8,128)(2,1)} %param.8), kind=kOutput, calls=%fused_computation.54 | convolution fusion | flops 3625189376 | bytes 19267584 | tf_op jit(solution)/shard_map/dot_general | solution.py:68
  99.6 48.1 %all-gather.3.cloned.1.call-done = bf16[2048,512]{1,0:T(8,128)(2,1)} async-done(((bf16[128,512]{1,0:T(8,128)(2,1)}), bf16[2048,512]{1,0:T(8,128)(2,1)}) %all-gather.3.cloned.1.call-update) | async-done | bytes 2097168 | tf_op jit(solution)/shard_map/all_gather | solution.py:86
  147.7 4.1 copy.45
  151.8 3.1 fusion.3
  155.0 3.3 copy-done.2
  158.2 3.0 convolution_convert_fusion.4
  161.2 39.5 %all-gather.5.cloned.1.call-done = bf16[2048,512]{1,0:T(8,128)(2,1)} async-done(((bf16[128,512]{1,0:T(8,128)(2,1)}), bf16[2048,512]{1,0:T(8,128)(2,1)}) %all-gather.5.cloned.1.call-update) | async-done | bytes 2097168 | tf_op jit(solution)/shard_map/all_gather | solution.py:87
  200.7 4.0 copy.48
  204.7 6.7 %fusion = (f32[8,128]{1,0:T(8,128)S(1)}, bf16[8,128,2048]{2,1,0:T(8,128)(2,1)S(1)}) fusion(f32[8,128]{1,0:T(8,128)S(1)} %get-tuple-element.44, f32[8,128,2048]{2,1,0:T(8,128)} %copy-done.2, bf16[128,8,64]{0,2,1:T(8,128)(2,1)S(1)} %bitcast.71, bf16[2048,8,64]{0,2,1:T(8,128)(2,1)} %bitcast.61), kind=kOutput, calls=%fused_computation.3 | convolution fusion | flops 281017344 | bytes 14819328 | tf_op jit(solution)/shard_map/ihe,jhe->hij/dot_general | solution.py:109
  211.4 5.9 %multiply_convert_fusion = bf16[8,64,2048]{2,1,0:T(8,128)(2,1)S(1)} fusion(bf16[128,8,64]{0,2,1:T(8,128)(2,1)S(1)} %bitcast.67, bf16[8,128,2048]{2,1,0:T(8,128)(2,1)S(1)} %get-tuple-element.47, f32[8,128]{1,0:T(8,128)S(1)} %get-tuple-element.46, f32[8,128,2048]{2,1,0:T(8,128)S(1)} %copy-done.3, f32[8,128]{1,0:T(8,128)S(1)} %get-tuple-element.44), kind=kOutput, calls=%fused_computation.11 | convolution fusion | flops 1623195648 | bytes 14819328 | tf_op jit(solution)/shard_map/hij,ihe->jhe/dot_general | solution.py:120
  217.3 2.5 pad_maximum_fusion
  219.9 6.4 %copy.59 = bf16[2048,1024]{1,0:T(8,128)(2,1)} copy(bf16[2048,1024]{0,1:T(8,128)(2,1)} %pad_maximum_fusion) | data formatting | bytes 8388608
  226.3 5.7 fusion.31
  233.5 11.9 %fusion.34 = bf16[8,64,128]{2,1,0:T(8,128)(2,1)S(1)} fusion(bf16[2048,8,64]{0,2,1:T(8,128)(2,1)} %bitcast.57, bf16[8,128,2048]{2,1,0:T(8,128)(2,1)} %copy-done.14, f32[8,128]{1,0:T(8,128)S(1)} %get-tuple-element.46, f32[8,128,2048]{2,1,0:T(8,128)} %copy-done.2, f32[8,128]{1,0:T(8,128)S(1)} %get-tuple-element.44), kind=kOutput, calls=%fused_computation.49 | convolution fusion | flops 1621229568 | bytes 14819328 | tf_op jit(solution)/shard_map/hij,jhe->ihe/dot_general | solution.py:114
  245.4 55.7 %reduce-scatter.16.cloned.1.call-done = bf16[128,1024]{1,0:T(8,128)(2,1)} async-done(((bf16[2048,1024]{1,0:T(8,128)(2,1)}), bf16[128,1024]{1,0:T(8,128)(2,1)}) %reduce-scatter.16.cloned.1.call-update) | async-done | bytes 262160
  304.1 2.8 multiply_reduce_fusion
  306.9 3.3 convolution_convert_fusion.2
  310.7 3.1 fusion.14
  315.7 2.7 copy.66
  322.8 3.8 collective-permute-start.4
  326.6 5.7 copy.56
  338.8 2.5 collective-permute-done.5
  344.6 10.8 %convolution_convert_fusion = bf16[6912,256]{1,0:T(8,128)(2,1)} fusion(bf16[1024,6912]{1,0:T(8,128)(2,1)} %reshape.89, bf16[1024,256]{1,0:T(8,128)(2,1)} %copy-done.6), kind=kOutput, calls=%fused_computation.2 | convolution fusion | flops 3625648128 | bytes 18219008 | tf_op jit(solution)/shard_map/vr,vc->rc/dot_general | solution.py:173
  355.4 26.0 %all-reduce.2 = f32[512]{0:T(512)S(1)} all-reduce(f32[512]{0:T(512)S(1)} %copy-done.12), channel_id=5, replica_groups=mesh['batch'=16,'gx'=4,'gy'=4] {'gx','gy'}, use_global_device_ids=true, to_apply=%region_10.11.clone | all-reduce | flops 512 | bytes 4096
  387.4 3.8 convolution_convert_fusion.7
  392.2 42.0 %reduce-scatter.12.cloned.1.call-done = bf16[32,1536]{1,0:T(8,128)(2,1)} async-done(((bf16[512,1536]{1,0:T(8,128)(2,1)}), bf16[32,1536]{1,0:T(8,128)(2,1)}) %reduce-scatter.12.cloned.1.call-update) | async-done | bytes 98320 | tf_op jit(solution)/shard_map/reduce_scatter | solution.py:195
  434.2 69.7 %reduce-scatter.10.cloned.1.call-done = bf16[128,512]{1,0:T(8,128)(2,1)} async-done(((bf16[2048,512]{1,0:T(8,128)(2,1)}), bf16[128,512]{1,0:T(8,128)(2,1)}) %reduce-scatter.10.cloned.1.call-update) | async-done | bytes 131088 | tf_op jit(solution)/shard_map/reduce_scatter | solution.py:192
  503.9 74.6 %reduce-scatter.8.cloned.1.call-done = bf16[432,256]{1,0:T(8,128)(2,1)} async-done(((bf16[6912,256]{1,0:T(8,128)(2,1)}), bf16[432,256]{1,0:T(8,128)(2,1)}) %reduce-scatter.8.cloned.1.call-update) | async-done | bytes 221200 | tf_op jit(solution)/shard_map/reduce_scatter | solution.py:189
  (149 shorter events, 74.6 us)
Async XLA Ops:
  7.2 85.7 %copy-start = (bf16[2048,512]{1,0:T(8,128)(2,1)S(1)}, bf16[2048,512]{1,0:T(8,128)(2,1)}, u32[]{:S(2)}) copy-start(bf16[2048,512]{1,0:T(8,128)(2,1)} %param.9) | copy-start | bytes 6291460
  7.2 140.6 %all-gather.3.cloned.1.call-start = ((), (), s32[]{:S(2)}) async-start(), calls=%async_computation.5 | async-start | bytes 2228224 | tf_op jit(solution)/shard_map/all_gather | solution.py:86
  8.2 6.5 %collective-permute-start = (bf16[1,16,4,256]{3,2,1,0:T(4,128)(2,1)S(1)}, bf16[1,16,4,256]{3,2,1,0:T(4,128)(2,1)S(1)}, u32[]{:S(2)}, u32[]{:S(2)}) collective-permute-start(bf16[1,16,4,256]{3,2,1,0:T(4,128)(2,1)S(1)} %get-tuple-element.36), channel_id=1, source_target_pairs={{0,4},{4,8},{8,12},{1,5},{5,9},{9,13},{2,6},{6,10},{10,14},{3,7},{... | collective-permute-start | bytes 98312 | tf_op jit(solution)/shard_map/ppermute | solution.py:18
  12.8 5.2 collective-permute-start.1
  14.7 27.6 %copy-start.1 = (bf16[16,16,4,256]{3,2,1,0:T(4,128)(2,1)S(1)}, bf16[16,16,4,256]{3,2,1,0:T(4,128)(2,1)}, u32[]{:S(2)}) copy-start(bf16[16,16,4,256]{3,2,1,0:T(4,128)(2,1)} %param.7) | copy-start | bytes 1572868
  18.1 4.4 collective-permute-start.2
  21.2 4.7 collective-permute-start.3
  81.1 12.6 %copy-start.10 = (f32[512]{0:T(512)S(1)}, f32[512]{0:T(512)}, u32[]{:S(2)}) copy-start(f32[512]{0:T(512)} %param.10) | copy-start | bytes 6148
  96.3 104.4 %all-gather.5.cloned.1.call-start = ((), (), s32[]{:S(2)}) async-start(), calls=%async_computation.6 | async-start | bytes 2228224 | tf_op jit(solution)/shard_map/all_gather | solution.py:87
  97.0 204.0 %reduce-scatter.16.cloned.1.call-start = ((), (), s32[]{:S(2)}) async-start(), calls=%async_computation.11 | async-start | bytes 4456448
  155.0 3.3 copy-start.2
  204.7 6.8 %copy-start.3 = (f32[8,128,2048]{2,1,0:T(8,128)S(1)}, f32[8,128,2048]{2,1,0:T(8,128)}, u32[]{:S(2)}) copy-start(f32[8,128,2048]{2,1,0:T(8,128)} %copy-done.2) | copy-start | bytes 25165828
  211.4 5.9 %copy-start.14 = (bf16[8,128,2048]{2,1,0:T(8,128)(2,1)}, bf16[8,128,2048]{2,1,0:T(8,128)(2,1)S(1)}, u32[]{:S(2)}) copy-start(bf16[8,128,2048]{2,1,0:T(8,128)(2,1)S(1)} %get-tuple-element.47) | copy-start | bytes 12582916
  211.4 5.9 %copy-start.7 = (bf16[8,64,2048]{2,1,0:T(8,128)(2,1)S(1)}, bf16[8,64,2048]{2,1,0:T(8,128)(2,1)}, u32[]{:S(2)}) copy-start(bf16[8,64,2048]{2,1,0:T(8,128)(2,1)} %convolution_convert_fusion.4) | copy-start | bytes 6291460
  226.3 166.0 %reduce-scatter.14.cloned.1.call-start = ((), (), s32[]{:S(2)}) async-start(), calls=%async_computation.10 | async-start | bytes 557056 | tf_op jit(solution)/shard_map/reduce_scatter | solution.py:198
  233.2 201.0 %reduce-scatter.12.cloned.1.call-start = ((), (), s32[]{:S(2)}) async-start(), calls=%async_computation.9 | async-start | bytes 1671168 | tf_op jit(solution)/shard_map/reduce_scatter | solution.py:195
  245.4 58.7 %copy-start.9 = (bf16[8,64,128]{2,1,0:T(8,128)(2,1)}, bf16[8,64,128]{2,1,0:T(8,128)(2,1)S(1)}, u32[]{:S(2)}) copy-start(bf16[8,64,128]{2,1,0:T(8,128)(2,1)S(1)} %fusion.34) | copy-start | bytes 393220
  304.0 199.9 %reduce-scatter.10.cloned.1.call-start = ((), (), s32[]{:S(2)}) async-start(), calls=%async_computation.8 | async-start | bytes 2228224 | tf_op jit(solution)/shard_map/reduce_scatter | solution.py:192
  306.8 3.4 copy-start.8
  306.9 3.4 copy-start.11
  310.2 268.3 %reduce-scatter.8.cloned.1.call-start = ((), (), s32[]{:S(2)}) async-start(), calls=%async_computation.7 | async-start | bytes 3760128 | tf_op jit(solution)/shard_map/reduce_scatter | solution.py:189
  313.8 18.5 %copy-start.13 = (u32[256]{0:T(256)S(1)}, u32[256]{0:T(256)}, u32[]{:S(2)}) copy-start(u32[256]{0:T(256)} %constant.27) | copy-start | bytes 3076
  321.9 0.8 copy-start.6
  322.8 14.8 %collective-permute-start.4 = (bf16[1,16,4,256]{3,1,2,0:T(8,128)(2,1)S(1)}, bf16[1,16,4,256]{3,1,2,0:T(8,128)(2,1)S(1)}, u32[]{:S(2)}, u32[]{:S(2)}) collective-permute-start(bf16[1,16,4,256]{3,1,2,0:T(8,128)(2,1)S(1)} %copy.50), channel_id=1, source_target_pairs={{0,4},{4,8},{8,12},{1,5},{5,9},{9,13},{2,6},{6,10},{10,14},{3,7},{... | collective-permute-start | bytes 98312 | tf_op jit(solution)/shard_map/ppermute | solution.py:18
  335.7 5.6 collective-permute-start.5
  342.0 40.0 %collective-permute-start.6 = (bf16[18,1,4,256]{3,1,2,0:T(2,128)(2,1)}, bf16[18,1,4,256]{3,1,2,0:T(2,128)(2,1)S(1)}, u32[]{:S(2)}, u32[]{:S(2)}) collective-permute-start(bf16[18,1,4,256]{3,1,2,0:T(2,128)(2,1)} %get-tuple-element.27), channel_id=1, source_target_pairs={{0,1},{1,2},{2,3},{4,5},{5,6},{6,7},{8,9},{9,10},{10,11},{12,13},{... | collective-permute-start | bytes 110600 | tf_op jit(solution)/shard_map/ppermute | solution.py:18
  343.3 12.1 %copy-start.12 = (f32[512]{0:T(512)S(1)}, f32[512]{0:T(512)}, u32[]{:S(2)}) copy-start(f32[512]{0:T(512)} %get-tuple-element.24) | copy-start | bytes 6148
  343.3 38.7 %collective-permute-start.7 = (bf16[18,1,4,256]{3,1,2,0:T(2,128)(2,1)S(1)}, bf16[18,1,4,256]{3,1,2,0:T(2,128)(2,1)S(1)}, u32[]{:S(2)}, u32[]{:S(2)}) collective-permute-start(bf16[18,1,4,256]{3,1,2,0:T(2,128)(2,1)S(1)} %get-tuple-element.28), channel_id=1, source_target_pairs={{1,0},{2,1},{3,2},{5,4},{6,5},{7,6},{9,8},{10,9},{11,10},{13,12},{... | collective-permute-start | bytes 110600 | tf_op jit(solution)/shard_map/ppermute | solution.py:21
  381.4 3.7 copy-start.4
  384.7 2.6 copy-start.5
Sparse Core Ops, SparseCore 0:
  96.4 51.2 all-gather.2
  150.1 50.5 all-gather.4
  226.4 74.5 reduce-scatter.15
  304.0 61.7 reduce-scatter.13
  368.7 65.4 reduce-scatter.11
  437.2 66.6 reduce-scatter.9
  507.1 71.3 reduce-scatter.7
where the time goes:
time: 593 us; the launch traced here: 586 us
  waiting for transfers between devices  338 us (57%)
  local copies, waits for them, and re-layouts  90.4 us (15%)
  matrix products  77.6 us (13%)
  blocking collectives  26 us (4%)
  starting transfers between devices  20.2 us (3%)
  other arithmetic  17.6 us (3%)
  between operations  15.6 us (3%)
    reduce_scatter x1, waiting for transfers between devices, local(): lax.psum_scatter(conv_part.astype(jnp.bfloat16), ('gx', 'gy'), scatter_di...  74.6 us
    reduce_scatter x1, waiting for transfers between devices, local(): lax.psum_scatter(down_part.astype(jnp.bfloat16), ('gx', 'gy'), scatter_di...  69.7 us
    unnamed x8, waiting for transfers between devices  56.5 us
    all_gather x1, waiting for transfers between devices, local(): lax.all_gather(local_keys, ('gx', 'gy'), axis=0, tiled=True)  48.1 us
    reduce_scatter x1, waiting for transfers between devices, local(): lax.psum_scatter(qkv_part.astype(jnp.bfloat16), ('gx', 'gy'), scatter_dim...  42 us
    all_gather x1, waiting for transfers between devices, local(): lax.all_gather(local_values, ('gx', 'gy'), axis=0, tiled=True)  39.5 us
    unnamed x74, local copies, waits for them, and re-layouts  38.3 us
    unnamed x1, blocking collectives  26 us
  transfers between devices with their start and end apart: 15, of which 9 were waited for; matrix products, arithmetic and copies ran while one was open for 14% of the time, Pallas kernels for 0%

commit v1 on v0

--- a/solution.py
+++ b/solution.py
@@ -82,10 +82,11 @@
     queries = qkv_rows[:, :model_width]
     local_keys = qkv_rows[:, model_width : 2 * model_width]
     local_values = qkv_rows[:, 2 * model_width :]
-    all_keys, all_values = (
-        lax.all_gather(local_keys, ("gx", "gy"), axis=0, tiled=True),
-        lax.all_gather(local_values, ("gx", "gy"), axis=0, tiled=True),
-    )
+    gathered = lax.all_gather(
+        qkv_rows[:, model_width:], ("gx", "gy"), axis=0, tiled=True
+    )
+    all_keys = gathered[:, :model_width]
+    all_values = gathered[:, model_width:]
     queries_h = queries.reshape(tok_count, H, HD)
     keys_h = all_keys.reshape(-1, H, HD)
     values_h = all_values.reshape(-1, H, HD)
@@ -152,7 +153,6 @@
     )
     d_hat = d_normed * norm_gain
     gain_part = jnp.sum(d_normed * normed, axis=0)
-    gain_sum = lax.psum_scatter(gain_part, ("gx", "gy"), scatter_dimension=0, tiled=True)
     d_trunk = cot_float + inverse_std * (
         d_hat
         - jnp.mean(d_hat, axis=-1, keepdims=True)
@@ -185,20 +185,37 @@
     grad_features = grad_features.reshape(extent_x, extent_y, extent_z, channels).astype(
         jnp.bfloat16
     )
-    conv_sum, down_sum, qkv_sum, out_sum = (
-        lax.psum_scatter(
-            conv_part.astype(jnp.bfloat16), ("gx", "gy"), scatter_dimension=0, tiled=True
-        ).astype(jnp.float32),
-        lax.psum_scatter(
-            down_part.astype(jnp.bfloat16), ("gx", "gy"), scatter_dimension=0, tiled=True
-        ).astype(jnp.float32),
-        lax.psum_scatter(
-            qkv_part.astype(jnp.bfloat16), ("gx", "gy"), scatter_dimension=0, tiled=True
-        ).astype(jnp.float32),
-        lax.psum_scatter(
-            out_part.astype(jnp.bfloat16), ("gx", "gy"), scatter_dimension=0, tiled=True
-        ).astype(jnp.float32),
-    )
+    groups = lax.axis_size(("gx", "gy"))
+    gain_rows = gain_part.reshape(groups, -1)
+    gain_high = gain_rows.astype(jnp.bfloat16)
+    gain_low = (gain_rows - gain_high.astype(jnp.float32)).astype(jnp.bfloat16)
+    gain_pair = jnp.concatenate([gain_high, gain_low], axis=1)
+    gain_pair = jnp.pad(gain_pair, ((0, 0), (0, 1024 - gain_pair.shape[1])))
+    pieces = [
+        conv_part.astype(jnp.bfloat16),
+        down_part.astype(jnp.bfloat16),
+        qkv_part.astype(jnp.bfloat16),
+        out_part.astype(jnp.bfloat16),
+    ]
+    shapes = [piece.shape for piece in pieces]
+    flat = [piece.reshape(groups, -1, 128) for piece in pieces] + [gain_pair.reshape(groups, -1, 128)]
+    heights = [piece.shape[1] for piece in flat]
+    joined = jnp.concatenate(flat, axis=1)
+    summed = lax.psum_scatter(
+        joined.reshape(-1, 128), ("gx", "gy"), scatter_dimension=0, tiled=True
+    )
+    summed = lax.optimization_barrier(summed)
+    results = []
+    offset = 0
+    for height in heights:
+        results.append(summed[offset : offset + height])
+        offset += height
+    conv_sum, down_sum, qkv_sum, out_sum = [
+        piece.reshape(shape[0] // groups, shape[1]) for piece, shape in zip(results[:4], shapes)
+    ]
+    gain_flat = results[4].reshape(-1).astype(jnp.float32)
+    half = gain_high.shape[1]
+    gain_sum = gain_flat[:half] + gain_flat[half : 2 * half]
     return (
         grad_features,
         conv_sum.astype(jnp.bfloat16),

time: 593 us -> 437 us (0.74)
  waiting for transfers between devices: 338 us -> 177 us
  local copies, waits for them, and re-layouts: 90.4 us -> 126 us
  blocking collectives: 26 us -> 0 us
  matrix products: 77.6 us -> 70.4 us
    reduce_scatter x4 -> x0, waiting for transfers between devices: 186 us -> none  [the longest x1 74.6 us: local(): lax.psum_scatter(conv_part.astype(jnp.bfloat16), ('gx', 'gy'), scatter_di...]
    unnamed x8 -> x5, waiting for transfers between devices: 56.5 us -> 118 us
    all_gather x2 -> x1, waiting for transfers between devices: 87.6 us -> 51.5 us  [local(): lax.all_gather(qkv_rows[:, model_width:], ('gx', 'gy'), axis=0, tiled=True)]
    unnamed x1 -> x0, blocking collectives: 26 us -> none
    reshape x0 -> x9, local copies, waits for them, and re-layouts: none -> 19.2 us  [the longest x4 16.2 us: local(): piece.reshape(groups, -1, 128)]
    slice x1 -> x8, local copies, waits for them, and re-layouts: 0.74 us -> 17.2 us  [the longest x2 8.51 us: local(): all_values = gathered[:, model_width:]]
    unnamed x74 -> x73, local copies, waits for them, and re-layouts: 38.3 us -> 46.5 us
    all_gather x2 -> x0, local copies, waits for them, and re-layouts: 8.06 us -> none  [the longest x1 4.1 us: local(): lax.all_gather(local_keys, ('gx', 'gy'), axis=0, tiled=True)]
  transfers between devices with their start and end apart: 15 -> 11, of which waited for: 9 -> 6; matrix products, arithmetic and copies ran while one was open for 14% -> 10% of each run, Pallas kernels for 0% -> 0%
where the time goes in v1:
time: 437 us; the launch traced here: 429 us
  waiting for transfers between devices  177 us (41%)
  local copies, waits for them, and re-layouts  126 us (29%)
  matrix products  70.4 us (16%)
  starting transfers between devices  21 us (5%)
  other arithmetic  19 us (4%)
  between operations  14.8 us (3%)
    unnamed x5, waiting for transfers between devices  118 us
    all_gather x1, waiting for transfers between devices, local(): lax.all_gather(qkv_rows[:, model_width:], ('gx', 'gy'), axis=0, tiled=True)  51.5 us
    unnamed x73, local copies, waits for them, and re-layouts  46.5 us
    reshape x1, local copies, waits for them, and re-layouts, gather_patches(): return joined.reshape(extent_x * extent_y * extent_z, 27 * channels)  22.5 us
    reshape x4, local copies, waits for them, and re-layouts, local(): piece.reshape(groups, -1, 128)  16.2 us
    ppermute x4, starting transfers between devices, padded_2(): lax.ppermute(lax.slice_in_dim(block, block.shape[dim] - width, None, axis...  14.1 us
    unnamed x17, other arithmetic  12.2 us
    dot_general x1, matrix products, local(): jnp.einsum('hij,jhe->ihe', d_scores, keys_h, precision=precise, preferred...  11.9 us
  transfers between devices with their start and end apart: 11, of which 6 were waited for; matrix products, arithmetic and copies ran while one was open for 10% of the time, Pallas kernels for 0%

profile of v1, /device:TPU:1, one launch (start us, length us, event | category | flops | bytes accessed | tf_op | source)
XLA Modules:
  0.0 428.9 jit_solution(12199377892580588452)
XLA Ops:
  8.2 4.6 %collective-permute-start = (bf16[1,16,4,256]{3,2,1,0:T(4,128)(2,1)S(1)}, bf16[1,16,4,256]{3,2,1,0:T(4,128)(2,1)S(1)}, u32[]{:S(2)}, u32[]{:S(2)}) collective-permute-start(bf16[1,16,4,256]{3,2,1,0:T(4,128)(2,1)S(1)} %get-tuple-element.40), channel_id=1, source_target_pairs={{0,4},{4,8},{8,12},{1,5},{5,9},{9,13},{2,6},{6,10},{10,14},{3,7},{... | collective-permute-start | bytes 98312 | tf_op jit(solution)/shard_map/ppermute | solution.py:18
  18.1 3.1 collective-permute-start.2
  22.5 3.4 collective-permute-done.3
  31.1 2.2 fusion.61
  58.3 22.5 %reshape.125 = bf16[1024,6912]{1,0:T(8,128)(2,1)} reshape(bf16[16,16,4,6912]{3,2,1,0:T(4,128)(2,1)} %slice_dynamic-update-slice_fusion.18) | data formatting | bytes 28311552 | tf_op jit(solution)/shard_map/reshape | solution.py:57
  80.8 10.9 %multiply_convert_fusion.2 = (bf16[1024,256]{1,0:T(8,128)(2,1)S(1)}, f32[1024,256]{1,0:T(8,128)}) fusion(bf16[1024,6912]{1,0:T(8,128)(2,1)} %reshape.125, bf16[6912,256]{1,0:T(8,128)(2,1)} %param.8), kind=kOutput, calls=%fused_computation.54 | convolution fusion | flops 3625189376 | bytes 19267584 | tf_op jit(solution)/shard_map/dot_general | solution.py:68
  99.3 51.5 %all-gather.2.cloned.1.call-done = bf16[2048,1024]{1,0:T(8,128)(2,1)} async-done(((bf16[128,1024]{1,0:T(8,128)(2,1)}), bf16[2048,1024]{1,0:T(8,128)(2,1)}) %all-gather.2.cloned.1.call-update) | async-done | bytes 4194320 | tf_op jit(solution)/shard_map/all_gather | solution.py:85
  150.8 4.5 %fusion.73 = (bf16[2048,512]{1,0:T(8,128)(2,1)}, bf16[2048,512]{1,0:T(8,128)(2,1)}) fusion(bf16[2048,1024]{1,0:T(8,128)(2,1)} %all-gather.2.cloned.1.call-done), kind=kLoop, calls=%fused_computation.169 | loop fusion | bytes 8388608 | tf_op jit(solution)/shard_map/slice | solution.py:89
  155.4 4.5 %copy.45 = bf16[2048,512]{0,1:T(8,128)(2,1)} copy(bf16[2048,512]{1,0:T(8,128)(2,1)} %get-tuple-element.30) | data formatting | bytes 4194304 | tf_op jit(solution)/shard_map/slice | solution.py:88
  159.8 4.0 copy.48
  163.8 3.1 fusion.3
  170.1 2.7 fusion
  172.9 5.9 %multiply_convert_fusion = bf16[8,64,2048]{2,1,0:T(8,128)(2,1)S(1)} fusion(bf16[128,8,64]{0,2,1:T(8,128)(2,1)S(1)} %bitcast.77, bf16[8,128,2048]{2,1,0:T(8,128)(2,1)S(1)} %get-tuple-element.48, f32[8,128]{1,0:T(8,128)S(1)} %get-tuple-element.47, f32[8,128,2048]{2,1,0:T(8,128)S(1)} %get-tuple-element.46, f32[8,128]{1,0:T(8,128)S(1)} %get-tuple-element.45), kind=kOutput, calls=%fused_computation.11 | convolution fusion | flops 1623195648 | bytes 14819328 | tf_op jit(solution)/shard_map/hij,ihe->jhe/dot_general | solution.py:121
  178.8 2.5 pad_maximum_fusion
  181.3 6.4 %copy.59 = bf16[2048,1024]{1,0:T(8,128)(2,1)} copy(bf16[2048,1024]{0,1:T(8,128)(2,1)} %pad_maximum_fusion) | data formatting | bytes 8388608
  187.9 5.7 %fusion.31 = bf16[8,64,128]{2,1,0:T(8,128)(2,1)S(1)} fusion(bf16[2048,8,64]{0,2,1:T(8,128)(2,1)} %bitcast.71, f32[8,128,2048]{2,1,0:T(8,128)} %copy-done.2, f32[8,128]{1,0:T(8,128)S(1)} %get-tuple-element.45), kind=kOutput, calls=%fused_computation.47 | convolution fusion | flops 274792448 | bytes 10620928 | tf_op jit(solution)/shard_map/hij,jhe->ihe/dot_general | solution.py:101
  195.1 11.9 %fusion.34 = bf16[8,64,128]{2,1,0:T(8,128)(2,1)S(1)} fusion(bf16[2048,8,64]{0,2,1:T(8,128)(2,1)} %bitcast.67, bf16[8,128,2048]{2,1,0:T(8,128)(2,1)} %copy-done.11, f32[8,128]{1,0:T(8,128)} %copy-done.12, f32[8,128,2048]{2,1,0:T(8,128)} %copy-done.2, f32[8,128]{1,0:T(8,128)S(1)} %get-tuple-element.45), kind=kOutput, calls=%fused_computation.49 | convolution fusion | flops 1621229568 | bytes 14819328 | tf_op jit(solution)/shard_map/hij,jhe->ihe/dot_general | solution.py:115
  207.0 54.1 %reduce-scatter.8.cloned.1.call-done = bf16[128,1024]{1,0:T(8,128)(2,1)} async-done(((bf16[2048,1024]{1,0:T(8,128)(2,1)}), bf16[128,1024]{1,0:T(8,128)(2,1)}) %reduce-scatter.8.cloned.1.call-update) | async-done | bytes 262160
  266.3 3.3 convolution_convert_fusion.2
  269.6 2.4 fusion.14
  272.0 4.3 %reshape.138 = bf16[16,384,128]{2,1,0:T(8,128)(2,1)} reshape(bf16[512,1536]{1,0:T(8,128)(2,1)} %convolution_convert_fusion.3) | data formatting | bytes 3145728 | tf_op jit(solution)/shard_map/reshape | solution.py:201
  276.3 4.4 %reshape.137 = bf16[16,512,128]{2,1,0:T(8,128)(2,1)} reshape(bf16[2048,512]{1,0:T(8,128)(2,1)} %convolution_convert_fusion.2) | data formatting | bytes 4194304 | tf_op jit(solution)/shard_map/reshape | solution.py:201
  282.5 2.7 copy.67
  289.5 10.7 %convolution_convert_fusion = bf16[6912,256]{1,0:T(8,128)(2,1)} fusion(bf16[1024,6912]{1,0:T(8,128)(2,1)} %reshape.125, bf16[1024,256]{1,0:T(8,128)(2,1)S(1)} %multiply_convert_fusion.1), kind=kOutput, calls=%fused_computation.2 | convolution fusion | flops 3625648128 | bytes 18219008 | tf_op jit(solution)/shard_map/vr,vc->rc/dot_general | solution.py:173
  300.2 6.4 %reshape.136 = bf16[16,864,128]{2,1,0:T(8,128)(2,1)} reshape(bf16[6912,256]{1,0:T(8,128)(2,1)} %convolution_convert_fusion) | data formatting | bytes 7077888 | tf_op jit(solution)/shard_map/reshape | solution.py:201
  306.6 4.5 %constant_dynamic-update-slice_fusion.12 = bf16[16,1896,128]{2,1,0:T(8,128)(2,1)} fusion(bf16[16,864,128]{2,1,0:T(8,128)(2,1)} %reshape.136), kind=kLoop, calls=%fused_computation.153 | loop fusion | bytes 7077888
  311.2 3.4 constant_dynamic-update-slice_fusion.11
  314.7 2.9 constant_dynamic-update-slice_fusion.10
  319.2 5.1 %collective-permute-start.4 = (bf16[1,16,4,256]{3,1,2,0:T(8,128)(2,1)S(1)}, bf16[1,16,4,256]{3,1,2,0:T(8,128)(2,1)S(1)}, u32[]{:S(2)}, u32[]{:S(2)}) collective-permute-start(bf16[1,16,4,256]{3,1,2,0:T(8,128)(2,1)S(1)} %copy.50), channel_id=1, source_target_pairs={{0,4},{4,8},{8,12},{1,5},{5,9},{9,13},{2,6},{6,10},{10,14},{3,7},{... | collective-permute-start | bytes 98312 | tf_op jit(solution)/shard_map/ppermute | solution.py:18
  334.1 5.8 %copy.56 = bf16[27,256,256]{2,1,0:T(8,128)(2,1)} copy(bf16[27,256,256]{1,2,0:T(8,128)(2,1)} %bitcast.69) | data formatting | bytes 7077888 | tf_op jit(solution)/shard_map/transpose | solution.py:181
  345.2 3.8 convolution_convert_fusion.7
  350.1 64.2 %reduce-scatter.10.cloned.1.call-done = bf16[1896,128]{1,0:T(8,128)(2,1)} async-done(((bf16[30336,128]{1,0:T(8,128)(2,1)}), bf16[1896,128]{1,0:T(8,128)(2,1)}) %reduce-scatter.10.cloned.1.call-update) | async-done | bytes 485392
  (155 shorter events, 86.7 us)
Async XLA Ops:
  7.2 85.5 %copy-start = (bf16[2048,512]{1,0:T(8,128)(2,1)S(1)}, bf16[2048,512]{1,0:T(8,128)(2,1)}, u32[]{:S(2)}) copy-start(bf16[2048,512]{1,0:T(8,128)(2,1)} %param.9) | copy-start | bytes 6291460
  7.2 143.7 %all-gather.2.cloned.1.call-start = ((), (), s32[]{:S(2)}) async-start(), calls=%async_computation.2 | async-start | bytes 4456448 | tf_op jit(solution)/shard_map/all_gather | solution.py:85
  8.2 6.5 %collective-permute-start = (bf16[1,16,4,256]{3,2,1,0:T(4,128)(2,1)S(1)}, bf16[1,16,4,256]{3,2,1,0:T(4,128)(2,1)S(1)}, u32[]{:S(2)}, u32[]{:S(2)}) collective-permute-start(bf16[1,16,4,256]{3,2,1,0:T(4,128)(2,1)S(1)} %get-tuple-element.40), channel_id=1, source_target_pairs={{0,4},{4,8},{8,12},{1,5},{5,9},{9,13},{2,6},{6,10},{10,14},{3,7},{... | collective-permute-start | bytes 98312 | tf_op jit(solution)/shard_map/ppermute | solution.py:18
  12.8 5.2 %collective-permute-start.1 = (bf16[1,16,4,256]{3,2,1,0:T(4,128)(2,1)S(1)}, bf16[1,16,4,256]{3,2,1,0:T(4,128)(2,1)S(1)}, u32[]{:S(2)}, u32[]{:S(2)}) collective-permute-start(bf16[1,16,4,256]{3,2,1,0:T(4,128)(2,1)S(1)} %get-tuple-element.39), channel_id=1, source_target_pairs={{4,0},{8,4},{12,8},{5,1},{9,5},{13,9},{6,2},{10,6},{14,10},{7,3},{... | collective-permute-start | bytes 98312 | tf_op jit(solution)/shard_map/ppermute | solution.py:21
  14.7 27.6 %copy-start.1 = (bf16[16,16,4,256]{3,2,1,0:T(4,128)(2,1)S(1)}, bf16[16,16,4,256]{3,2,1,0:T(4,128)(2,1)}, u32[]{:S(2)}) copy-start(bf16[16,16,4,256]{3,2,1,0:T(4,128)(2,1)} %param.7) | copy-start | bytes 1572868
  18.1 4.4 %collective-permute-start.2 = (bf16[18,1,4,256]{3,2,1,0:T(4,128)(2,1)S(1)}, bf16[18,1,4,256]{3,2,1,0:T(4,128)(2,1)S(1)}, u32[]{:S(2)}, u32[]{:S(2)}) collective-permute-start(bf16[18,1,4,256]{3,2,1,0:T(4,128)(2,1)S(1)} %get-tuple-element.33), channel_id=1, source_target_pairs={{0,1},{1,2},{2,3},{4,5},{5,6},{6,7},{8,9},{9,10},{10,11},{12,13},{... | collective-permute-start | bytes 110600 | tf_op jit(solution)/shard_map/ppermute | solution.py:18
  21.2 4.7 %collective-permute-start.3 = (bf16[18,1,4,256]{3,2,1,0:T(4,128)(2,1)S(1)}, bf16[18,1,4,256]{3,2,1,0:T(4,128)(2,1)S(1)}, u32[]{:S(2)}, u32[]{:S(2)}) collective-permute-start(bf16[18,1,4,256]{3,2,1,0:T(4,128)(2,1)S(1)} %get-tuple-element.34), channel_id=1, source_target_pairs={{1,0},{2,1},{3,2},{5,4},{6,5},{7,6},{9,8},{10,9},{11,10},{13,12},{... | collective-permute-start | bytes 110600 | tf_op jit(solution)/shard_map/ppermute | solution.py:21
  80.8 12.6 %copy-start.10 = (f32[512]{0:T(512)S(1)}, f32[512]{0:T(512)}, u32[]{:S(2)}) copy-start(f32[512]{0:T(512)} %param.10) | copy-start | bytes 6148
  96.1 165.1 %reduce-scatter.8.cloned.1.call-start = ((), (), s32[]{:S(2)}) async-start(), calls=%async_computation.3 | async-start | bytes 4456448
  159.8 7.1 %copy-start.9 = (bf16[128,512]{0,1:T(8,128)(2,1)S(1)}, bf16[128,512]{0,1:T(8,128)(2,1)}, u32[]{:S(2)}) copy-start(bf16[128,512]{0,1:T(8,128)(2,1)} %copy.47) | copy-start | bytes 393220
  167.0 5.9 %copy-start.2 = (f32[8,128,2048]{2,1,0:T(8,128)}, f32[8,128,2048]{2,1,0:T(8,128)S(1)}, u32[]{:S(2)}) copy-start(f32[8,128,2048]{2,1,0:T(8,128)S(1)} %get-tuple-element.46) | copy-start | bytes 25165828
  167.0 3.2 copy-start.7
  172.8 5.9 %copy-start.11 = (bf16[8,128,2048]{2,1,0:T(8,128)(2,1)}, bf16[8,128,2048]{2,1,0:T(8,128)(2,1)S(1)}, u32[]{:S(2)}) copy-start(bf16[8,128,2048]{2,1,0:T(8,128)(2,1)S(1)} %get-tuple-element.48) | copy-start | bytes 12582916
  172.9 5.9 %copy-start.12 = (f32[8,128]{1,0:T(8,128)}, f32[8,128]{1,0:T(8,128)S(1)}, u32[]{:S(2)}) copy-start(f32[8,128]{1,0:T(8,128)S(1)} %get-tuple-element.47) | copy-start | bytes 12292
  187.7 226.6 %reduce-scatter.10.cloned.1.call-start = ((), (), s32[]{:S(2)}) async-start(), calls=%async_computation.4 | async-start | bytes 8251392
  288.7 0.8 copy-start.5
  306.6 11.0 %copy-start.8 = (bf16[16,128,128]{2,1,0:T(8,128)(2,1)S(1)}, bf16[16,128,128]{2,1,0:T(8,128)(2,1)}, u32[]{:S(2)}) copy-start(bf16[16,128,128]{2,1,0:T(8,128)(2,1)} %reshape.139) | copy-start | bytes 1572868
  311.1 8.1 %copy-start.6 = (bf16[1024,256]{1,0:T(8,128)(2,1)S(1)}, bf16[1024,256]{1,0:T(8,128)(2,1)}, u32[]{:S(2)}) copy-start(bf16[1024,256]{1,0:T(8,128)(2,1)} %copy-done.5) | copy-start | bytes 1572868
  319.2 8.0 %collective-permute-start.4 = (bf16[1,16,4,256]{3,1,2,0:T(8,128)(2,1)S(1)}, bf16[1,16,4,256]{3,1,2,0:T(8,128)(2,1)S(1)}, u32[]{:S(2)}, u32[]{:S(2)}) collective-permute-start(bf16[1,16,4,256]{3,1,2,0:T(8,128)(2,1)S(1)} %copy.50), channel_id=1, source_target_pairs={{0,4},{4,8},{8,12},{1,5},{5,9},{9,13},{2,6},{6,10},{10,14},{3,7},{... | collective-permute-start | bytes 98312 | tf_op jit(solution)/shard_map/ppermute | solution.py:18
  325.3 5.2 %collective-permute-start.5 = (bf16[1,16,4,256]{3,1,2,0:T(8,128)(2,1)S(1)}, bf16[1,16,4,256]{3,1,2,0:T(8,128)(2,1)S(1)}, u32[]{:S(2)}, u32[]{:S(2)}) collective-permute-start(bf16[1,16,4,256]{3,1,2,0:T(8,128)(2,1)S(1)} %copy.51), channel_id=1, source_target_pairs={{4,0},{8,4},{12,8},{5,1},{9,5},{13,9},{6,2},{10,6},{14,10},{7,3},{... | collective-permute-start | bytes 98312 | tf_op jit(solution)/shard_map/ppermute | solution.py:21
  331.2 8.6 %collective-permute-start.6 = (bf16[18,1,4,256]{3,1,2,0:T(2,128)(2,1)}, bf16[18,1,4,256]{3,1,2,0:T(2,128)(2,1)S(1)}, u32[]{:S(2)}, u32[]{:S(2)}) collective-permute-start(bf16[18,1,4,256]{3,1,2,0:T(2,128)(2,1)} %get-tuple-element.31), channel_id=1, source_target_pairs={{0,1},{1,2},{2,3},{4,5},{5,6},{6,7},{8,9},{9,10},{10,11},{12,13},{... | collective-permute-start | bytes 110600 | tf_op jit(solution)/shard_map/ppermute | solution.py:18
  332.5 7.3 %collective-permute-start.7 = (bf16[18,1,4,256]{3,1,2,0:T(2,128)(2,1)S(1)}, bf16[18,1,4,256]{3,1,2,0:T(2,128)(2,1)S(1)}, u32[]{:S(2)}, u32[]{:S(2)}) collective-permute-start(bf16[18,1,4,256]{3,1,2,0:T(2,128)(2,1)S(1)} %get-tuple-element.32), channel_id=1, source_target_pairs={{1,0},{2,1},{3,2},{5,4},{6,5},{7,6},{9,8},{10,9},{11,10},{13,12},{... | collective-permute-start | bytes 110600 | tf_op jit(solution)/shard_map/ppermute | solution.py:21
  339.9 3.1 copy-start.3
  342.6 2.6 copy-start.4
Sparse Core Ops, SparseCore 0:
  96.2 54.6 all-gather.1
  187.8 73.2 reduce-scatter.7
  319.3 94.9 reduce-scatter.9

commit v2 on v1

--- a/solution.py
+++ b/solution.py
@@ -128,18 +128,18 @@
         * score_scale
     )
     value_term = jnp.einsum("hij,ihe->jhe", probs_b, d_att_h, preferred_element_type=jnp.float32)
-    key_sums = lax.psum_scatter(
-        jnp.concatenate(
-            [
-                key_term.reshape(tok_count * lax.axis_size(("gx", "gy")), model_width),
-                value_term.reshape(tok_count * lax.axis_size(("gx", "gy")), model_width),
-            ],
-            axis=1,
-        ).astype(jnp.bfloat16),
-        ("gx", "gy"),
-        scatter_dimension=0,
-        tiled=True,
-    ).astype(jnp.float32)
+    groups = lax.axis_size(("gx", "gy"))
+    key_parts = jnp.concatenate(
+        [
+            key_term.reshape(tok_count * groups, model_width),
+            value_term.reshape(tok_count * groups, model_width),
+        ],
+        axis=1,
+    ).astype(jnp.bfloat16)
+    key_parts = lax.all_to_all(key_parts, ("gx", "gy"), 0, 0, tiled=True)
+    key_sums = jnp.sum(
+        key_parts.reshape(groups, tok_count, 2 * model_width).astype(jnp.float32), axis=0
+    )
     d_keys = key_sums[:, :model_width].astype(jnp.bfloat16)
     d_values = key_sums[:, model_width:].astype(jnp.bfloat16)
     d_qkv = jnp.concatenate(

time: 437 us -> 416 us (0.952)
  waiting for transfers between devices: 177 us -> 159 us
  local copies, waits for them, and re-layouts: 126 us -> 117 us
    unnamed x5 -> x3, waiting for transfers between devices: 118 us -> 64 us
    all_to_all x0 -> x1, waiting for transfers between devices: none -> 35.8 us  [local(): key_parts = lax.all_to_all(key_parts, ('gx', 'gy'), 0, 0, tiled=True)]
    unnamed x73 -> x77, local copies, waits for them, and re-layouts: 46.5 us -> 37.3 us
    all_to_all x0 -> x1, starting transfers between devices: none -> 5.44 us  [local(): key_parts = lax.all_to_all(key_parts, ('gx', 'gy'), 0, 0, tiled=True)]
  transfers between devices with their start and end apart: 11 -> 11, of which waited for: 6 -> 7; matrix products, arithmetic and copies ran while one was open for 10% -> 10% of each run, Pallas kernels for 0% -> 0%
where the time goes in v2:
time: 416 us; the launch traced here: 408 us
  waiting for transfers between devices  159 us (38%)
  local copies, waits for them, and re-layouts  117 us (28%)
  matrix products  70.3 us (17%)
  starting transfers between devices  24.3 us (6%)
  other arithmetic  21.7 us (5%)
  between operations  14.9 us (4%)
    unnamed x3, waiting for transfers between devices  64 us
    all_gather x1, waiting for transfers between devices, local(): lax.all_gather(qkv_rows[:, model_width:], ('gx', 'gy'), axis=0, tiled=True)  51.6 us
    unnamed x77, local copies, waits for them, and re-layouts  37.3 us
    all_to_all x1, waiting for transfers between devices, local(): key_parts = lax.all_to_all(key_parts, ('gx', 'gy'), 0, 0, tiled=True)  35.8 us
    reshape x1, local copies, waits for them, and re-layouts, gather_patches(): return joined.reshape(extent_x * extent_y * extent_z, 27 * channels)  22.4 us
    reshape x4, local copies, waits for them, and re-layouts, local(): piece.reshape(groups, -1, 128)  16.2 us
    unnamed x17, other arithmetic  12.1 us
    dot_general x1, matrix products, local(): jnp.einsum('hij,jhe->ihe', d_scores, keys_h, precision=precise, preferred...  11.9 us
  transfers between devices with their start and end apart: 11, of which 7 were waited for; matrix products, arithmetic and copies ran while one was open for 10% of the time, Pallas kernels for 0%

profile of v2, /device:TPU:1, one launch (start us, length us, event | category | flops | bytes accessed | tf_op | source)
XLA Modules:
  0.0 407.5 jit_solution(9080338234835893111)
XLA Ops:
  8.2 4.6 %collective-permute-start = (bf16[1,16,4,256]{3,2,1,0:T(4,128)(2,1)S(1)}, bf16[1,16,4,256]{3,2,1,0:T(4,128)(2,1)S(1)}, u32[]{:S(2)}, u32[]{:S(2)}) collective-permute-start(bf16[1,16,4,256]{3,2,1,0:T(4,128)(2,1)S(1)} %get-tuple-element.40), channel_id=1, source_target_pairs={{0,4},{4,8},{8,12},{1,5},{5,9},{9,13},{2,6},{6,10},{10,14},{3,7},{... | collective-permute-start | bytes 98312 | tf_op jit(solution)/shard_map/ppermute | solution.py:18
  18.1 3.1 collective-permute-start.2
  22.5 3.4 collective-permute-done.3
  31.1 2.1 fusion.61
  58.3 22.4 %reshape.129 = bf16[1024,6912]{1,0:T(8,128)(2,1)} reshape(bf16[16,16,4,6912]{3,2,1,0:T(4,128)(2,1)} %slice_dynamic-update-slice_fusion.18) | data formatting | bytes 28311552 | tf_op jit(solution)/shard_map/reshape | solution.py:57
  80.7 10.9 %multiply_convert_fusion.2 = (bf16[1024,256]{1,0:T(8,128)(2,1)S(1)}, f32[1024,256]{1,0:T(8,128)}) fusion(bf16[1024,6912]{1,0:T(8,128)(2,1)} %reshape.129, bf16[6912,256]{1,0:T(8,128)(2,1)} %param.8), kind=kOutput, calls=%fused_computation.54 | convolution fusion | flops 3625189376 | bytes 19267584 | tf_op jit(solution)/shard_map/dot_general | solution.py:68
  99.1 51.6 %all-gather.2.cloned.1.call-done = bf16[2048,1024]{1,0:T(8,128)(2,1)} async-done(((bf16[128,1024]{1,0:T(8,128)(2,1)}), bf16[2048,1024]{1,0:T(8,128)(2,1)}) %all-gather.2.cloned.1.call-update) | async-done | bytes 4194320 | tf_op jit(solution)/shard_map/all_gather | solution.py:85
  150.7 4.5 %fusion.73 = (bf16[2048,512]{1,0:T(8,128)(2,1)}, bf16[2048,512]{1,0:T(8,128)(2,1)}) fusion(bf16[2048,1024]{1,0:T(8,128)(2,1)} %all-gather.2.cloned.1.call-done), kind=kLoop, calls=%fused_computation.169 | loop fusion | bytes 8388608 | tf_op jit(solution)/shard_map/slice | solution.py:89
  155.2 3.9 copy.47
  159.2 4.0 copy.50
  163.2 3.1 fusion.3
  169.5 2.7 fusion
  172.2 5.9 %multiply_convert_fusion = bf16[8,64,2048]{2,1,0:T(8,128)(2,1)S(1)} fusion(bf16[128,8,64]{0,2,1:T(8,128)(2,1)S(1)} %bitcast.83, bf16[8,128,2048]{2,1,0:T(8,128)(2,1)S(1)} %get-tuple-element.48, f32[8,128]{1,0:T(8,128)S(1)} %get-tuple-element.47, f32[8,128,2048]{2,1,0:T(8,128)S(1)} %get-tuple-element.46, f32[8,128]{1,0:T(8,128)S(1)} %get-tuple-element.45), kind=kOutput, calls=%fused_computation.11 | convolution fusion | flops 1623195648 | bytes 14819328 | tf_op jit(solution)/shard_map/hij,ihe->jhe/dot_general | solution.py:121
  180.5 2.5 pad_maximum_fusion
  182.9 5.4 %all-to-all-start = ((bf16[16,128,1024]{1,2,0:T(8,128)(2,1)}), bf16[16,128,1024]{1,2,0:T(8,128)(2,1)}, u32[]{:S(2)}, u32[]{:S(2)}) async-start(bf16[16,128,1024]{1,2,0:T(8,128)(2,1)} %pad_maximum_fusion), calls=%async_computation | async-start | bytes 8388608 | tf_op jit(solution)/shard_map/all_to_all | solution.py:139
  188.8 5.7 %fusion.31 = bf16[8,64,128]{2,1,0:T(8,128)(2,1)S(1)} fusion(bf16[2048,8,64]{0,2,1:T(8,128)(2,1)} %bitcast.77, f32[8,128,2048]{2,1,0:T(8,128)} %copy-done.2, f32[8,128]{1,0:T(8,128)S(1)} %get-tuple-element.45), kind=kOutput, calls=%fused_computation.47 | convolution fusion | flops 274792448 | bytes 10620928 | tf_op jit(solution)/shard_map/hij,jhe->ihe/dot_general | solution.py:101
  196.0 11.9 %fusion.34 = bf16[8,64,128]{2,1,0:T(8,128)(2,1)S(1)} fusion(bf16[2048,8,64]{0,2,1:T(8,128)(2,1)} %bitcast.71, bf16[8,128,2048]{2,1,0:T(8,128)(2,1)} %copy-done.13, f32[8,128]{1,0:T(8,128)} %copy-done.14, f32[8,128,2048]{2,1,0:T(8,128)} %copy-done.2, f32[8,128]{1,0:T(8,128)S(1)} %get-tuple-element.45), kind=kOutput, calls=%fused_computation.49 | convolution fusion | flops 1621229568 | bytes 14819328 | tf_op jit(solution)/shard_map/hij,jhe->ihe/dot_general | solution.py:115
  207.9 35.8 %all-to-all-done = bf16[16,128,1024]{1,2,0:T(8,128)(2,1)} async-done(((bf16[16,128,1024]{1,2,0:T(8,128)(2,1)}), bf16[16,128,1024]{1,2,0:T(8,128)(2,1)}, u32[]{:S(2)}, u32[]{:S(2)}) %all-to-all-start) | async-done | bytes 4194336 | tf_op jit(solution)/shard_map/all_to_all | solution.py:139
  243.6 2.9 reduce
  246.5 2.2 multiply_reduce_fusion
  250.5 3.3 convolution_convert_fusion.2
  253.8 2.4 fusion.14
  256.3 4.3 %reshape.140 = bf16[16,384,128]{2,1,0:T(8,128)(2,1)} reshape(bf16[512,1536]{1,0:T(8,128)(2,1)} %convolution_convert_fusion.3) | data formatting | bytes 3145728 | tf_op jit(solution)/shard_map/reshape | solution.py:201
  260.7 4.4 %reshape.139 = bf16[16,512,128]{2,1,0:T(8,128)(2,1)} reshape(bf16[2048,512]{1,0:T(8,128)(2,1)} %convolution_convert_fusion.2) | data formatting | bytes 4194304 | tf_op jit(solution)/shard_map/reshape | solution.py:201
  266.9 2.7 copy.73
  273.9 10.7 %convolution_convert_fusion = bf16[6912,256]{1,0:T(8,128)(2,1)} fusion(bf16[1024,6912]{1,0:T(8,128)(2,1)} %reshape.129, bf16[1024,256]{1,0:T(8,128)(2,1)S(1)} %multiply_convert_fusion.1), kind=kOutput, calls=%fused_computation.2 | convolution fusion | flops 3625648128 | bytes 18219008 | tf_op jit(solution)/shard_map/vr,vc->rc/dot_general | solution.py:173
  284.6 6.4 %reshape.138 = bf16[16,864,128]{2,1,0:T(8,128)(2,1)} reshape(bf16[6912,256]{1,0:T(8,128)(2,1)} %convolution_convert_fusion) | data formatting | bytes 7077888 | tf_op jit(solution)/shard_map/reshape | solution.py:201
  291.0 4.5 %constant_dynamic-update-slice_fusion.12 = bf16[16,1896,128]{2,1,0:T(8,128)(2,1)} fusion(bf16[16,864,128]{2,1,0:T(8,128)(2,1)} %reshape.138), kind=kLoop, calls=%fused_computation.153 | loop fusion | bytes 7077888
  300.2 2.8 collective-permute-start.4
  312.8 5.8 %copy.61 = bf16[27,256,256]{2,1,0:T(8,128)(2,1)} copy(bf16[27,256,256]{1,2,0:T(8,128)(2,1)} %bitcast.75) | data formatting | bytes 7077888 | tf_op jit(solution)/shard_map/transpose | solution.py:181
  323.9 3.8 convolution_convert_fusion.7
  328.8 64.0 %reduce-scatter.5.cloned.1.call-done = bf16[1896,128]{1,0:T(8,128)(2,1)} async-done(((bf16[30336,128]{1,0:T(8,128)(2,1)}), bf16[1896,128]{1,0:T(8,128)(2,1)}) %reduce-scatter.5.cloned.1.call-update) | async-done | bytes 485392
  (161 shorter events, 89.1 us)
Async XLA Ops:
  7.2 85.4 %copy-start = (bf16[2048,512]{1,0:T(8,128)(2,1)S(1)}, bf16[2048,512]{1,0:T(8,128)(2,1)}, u32[]{:S(2)}) copy-start(bf16[2048,512]{1,0:T(8,128)(2,1)} %param.9) | copy-start | bytes 6291460
  7.2 143.5 %all-gather.2.cloned.1.call-start = ((), (), s32[]{:S(2)}) async-start(), calls=%async_computation.2 | async-start | bytes 4456448 | tf_op jit(solution)/shard_map/all_gather | solution.py:85
  8.2 6.5 %collective-permute-start = (bf16[1,16,4,256]{3,2,1,0:T(4,128)(2,1)S(1)}, bf16[1,16,4,256]{3,2,1,0:T(4,128)(2,1)S(1)}, u32[]{:S(2)}, u32[]{:S(2)}) collective-permute-start(bf16[1,16,4,256]{3,2,1,0:T(4,128)(2,1)S(1)} %get-tuple-element.40), channel_id=1, source_target_pairs={{0,4},{4,8},{8,12},{1,5},{5,9},{9,13},{2,6},{6,10},{10,14},{3,7},{... | collective-permute-start | bytes 98312 | tf_op jit(solution)/shard_map/ppermute | solution.py:18
  12.8 5.2 %collective-permute-start.1 = (bf16[1,16,4,256]{3,2,1,0:T(4,128)(2,1)S(1)}, bf16[1,16,4,256]{3,2,1,0:T(4,128)(2,1)S(1)}, u32[]{:S(2)}, u32[]{:S(2)}) collective-permute-start(bf16[1,16,4,256]{3,2,1,0:T(4,128)(2,1)S(1)} %get-tuple-element.39), channel_id=1, source_target_pairs={{4,0},{8,4},{12,8},{5,1},{9,5},{13,9},{6,2},{10,6},{14,10},{7,3},{... | collective-permute-start | bytes 98312 | tf_op jit(solution)/shard_map/ppermute | solution.py:21
  14.7 27.6 %copy-start.1 = (bf16[16,16,4,256]{3,2,1,0:T(4,128)(2,1)S(1)}, bf16[16,16,4,256]{3,2,1,0:T(4,128)(2,1)}, u32[]{:S(2)}) copy-start(bf16[16,16,4,256]{3,2,1,0:T(4,128)(2,1)} %param.7) | copy-start | bytes 1572868
  18.1 4.4 %collective-permute-start.2 = (bf16[18,1,4,256]{3,2,1,0:T(4,128)(2,1)S(1)}, bf16[18,1,4,256]{3,2,1,0:T(4,128)(2,1)S(1)}, u32[]{:S(2)}, u32[]{:S(2)}) collective-permute-start(bf16[18,1,4,256]{3,2,1,0:T(4,128)(2,1)S(1)} %get-tuple-element.33), channel_id=1, source_target_pairs={{0,1},{1,2},{2,3},{4,5},{5,6},{6,7},{8,9},{9,10},{10,11},{12,13},{... | collective-permute-start | bytes 110600 | tf_op jit(solution)/shard_map/ppermute | solution.py:18
  21.2 4.7 %collective-permute-start.3 = (bf16[18,1,4,256]{3,2,1,0:T(4,128)(2,1)S(1)}, bf16[18,1,4,256]{3,2,1,0:T(4,128)(2,1)S(1)}, u32[]{:S(2)}, u32[]{:S(2)}) collective-permute-start(bf16[18,1,4,256]{3,2,1,0:T(4,128)(2,1)S(1)} %get-tuple-element.34), channel_id=1, source_target_pairs={{1,0},{2,1},{3,2},{5,4},{6,5},{7,6},{9,8},{10,9},{11,10},{13,12},{... | collective-permute-start | bytes 110600 | tf_op jit(solution)/shard_map/ppermute | solution.py:21
  80.7 12.6 %copy-start.12 = (f32[512]{0:T(512)S(1)}, f32[512]{0:T(512)}, u32[]{:S(2)}) copy-start(f32[512]{0:T(512)} %param.10) | copy-start | bytes 6148
  159.2 7.1 %copy-start.11 = (bf16[128,512]{0,1:T(8,128)(2,1)S(1)}, bf16[128,512]{0,1:T(8,128)(2,1)}, u32[]{:S(2)}) copy-start(bf16[128,512]{0,1:T(8,128)(2,1)} %copy.49) | copy-start | bytes 393220
  166.3 5.9 %copy-start.2 = (f32[8,128,2048]{2,1,0:T(8,128)}, f32[8,128,2048]{2,1,0:T(8,128)S(1)}, u32[]{:S(2)}) copy-start(f32[8,128,2048]{2,1,0:T(8,128)S(1)} %get-tuple-element.46) | copy-start | bytes 25165828
  166.3 3.2 copy-start.9
  172.2 5.9 %copy-start.13 = (bf16[8,128,2048]{2,1,0:T(8,128)(2,1)}, bf16[8,128,2048]{2,1,0:T(8,128)(2,1)S(1)}, u32[]{:S(2)}) copy-start(bf16[8,128,2048]{2,1,0:T(8,128)(2,1)S(1)} %get-tuple-element.48) | copy-start | bytes 12582916
  172.2 5.9 %copy-start.14 = (f32[8,128]{1,0:T(8,128)}, f32[8,128]{1,0:T(8,128)S(1)}, u32[]{:S(2)}) copy-start(f32[8,128]{1,0:T(8,128)S(1)} %get-tuple-element.47) | copy-start | bytes 12292
  182.9 60.7 %all-to-all-start = ((bf16[16,128,1024]{1,2,0:T(8,128)(2,1)}), bf16[16,128,1024]{1,2,0:T(8,128)(2,1)}, u32[]{:S(2)}, u32[]{:S(2)}) async-start(bf16[16,128,1024]{1,2,0:T(8,128)(2,1)} %pad_maximum_fusion), calls=%async_computation | async-start | bytes 8388608 | tf_op jit(solution)/shard_map/all_to_all | solution.py:139
  188.4 204.4 %reduce-scatter.5.cloned.1.call-start = ((), (), s32[]{:S(2)}) async-start(), calls=%async_computation.3 | async-start | bytes 8251392
  273.1 0.8 copy-start.7
  291.0 4.5 %copy-start.3 = (bf16[16,512,128]{2,1,0:T(8,128)(2,1)S(1)}, bf16[16,512,128]{2,1,0:T(8,128)(2,1)}, u32[]{:S(2)}) copy-start(bf16[16,512,128]{2,1,0:T(8,128)(2,1)} %reshape.139) | copy-start | bytes 6291460
  291.0 6.2 %copy-start.4 = (bf16[16,384,128]{2,1,0:T(8,128)(2,1)S(1)}, bf16[16,384,128]{2,1,0:T(8,128)(2,1)}, u32[]{:S(2)}) copy-start(bf16[16,384,128]{2,1,0:T(8,128)(2,1)} %reshape.140) | copy-start | bytes 4718596
  291.0 7.7 %copy-start.10 = (bf16[16,128,128]{2,1,0:T(8,128)(2,1)S(1)}, bf16[16,128,128]{2,1,0:T(8,128)(2,1)}, u32[]{:S(2)}) copy-start(bf16[16,128,128]{2,1,0:T(8,128)(2,1)} %reshape.141) | copy-start | bytes 1572868
  295.5 4.7 %copy-start.8 = (bf16[1024,256]{1,0:T(8,128)(2,1)S(1)}, bf16[1024,256]{1,0:T(8,128)(2,1)}, u32[]{:S(2)}) copy-start(bf16[1024,256]{1,0:T(8,128)(2,1)} %copy-done.7) | copy-start | bytes 1572868
  300.2 5.7 %collective-permute-start.4 = (bf16[1,16,4,256]{3,1,2,0:T(8,128)(2,1)S(1)}, bf16[1,16,4,256]{3,1,2,0:T(8,128)(2,1)S(1)}, u32[]{:S(2)}, u32[]{:S(2)}) collective-permute-start(bf16[1,16,4,256]{3,1,2,0:T(8,128)(2,1)S(1)} %copy.55), channel_id=1, source_target_pairs={{0,4},{4,8},{8,12},{1,5},{5,9},{9,13},{2,6},{6,10},{10,14},{3,7},{... | collective-permute-start | bytes 98312 | tf_op jit(solution)/shard_map/ppermute | solution.py:18
  304.0 5.2 %collective-permute-start.5 = (bf16[1,16,4,256]{3,1,2,0:T(8,128)(2,1)S(1)}, bf16[1,16,4,256]{3,1,2,0:T(8,128)(2,1)S(1)}, u32[]{:S(2)}, u32[]{:S(2)}) collective-permute-start(bf16[1,16,4,256]{3,1,2,0:T(8,128)(2,1)S(1)} %copy.56), channel_id=1, source_target_pairs={{4,0},{8,4},{12,8},{5,1},{9,5},{13,9},{6,2},{10,6},{14,10},{7,3},{... | collective-permute-start | bytes 98312 | tf_op jit(solution)/shard_map/ppermute | solution.py:21
  310.0 8.6 %collective-permute-start.6 = (bf16[18,1,4,256]{3,1,2,0:T(2,128)(2,1)}, bf16[18,1,4,256]{3,1,2,0:T(2,128)(2,1)S(1)}, u32[]{:S(2)}, u32[]{:S(2)}) collective-permute-start(bf16[18,1,4,256]{3,1,2,0:T(2,128)(2,1)} %get-tuple-element.31), channel_id=1, source_target_pairs={{0,1},{1,2},{2,3},{4,5},{5,6},{6,7},{8,9},{9,10},{10,11},{12,13},{... | collective-permute-start | bytes 110600 | tf_op jit(solution)/shard_map/ppermute | solution.py:18
  311.3 7.3 %collective-permute-start.7 = (bf16[18,1,4,256]{3,1,2,0:T(2,128)(2,1)S(1)}, bf16[18,1,4,256]{3,1,2,0:T(2,128)(2,1)S(1)}, u32[]{:S(2)}, u32[]{:S(2)}) collective-permute-start(bf16[18,1,4,256]{3,1,2,0:T(2,128)(2,1)S(1)} %get-tuple-element.32), channel_id=1, source_target_pairs={{1,0},{2,1},{3,2},{5,4},{6,5},{7,6},{9,8},{10,9},{11,10},{13,12},{... | collective-permute-start | bytes 110600 | tf_op jit(solution)/shard_map/ppermute | solution.py:21
  318.5 3.2 copy-start.5
  321.3 2.6 copy-start.6
Sparse Core Ops, SparseCore 0:
  96.0 54.6 all-gather.1
  300.3 92.4 reduce-scatter.4
